TPU v7x, 128 devices: a whole 4x4x4 slice. The times are simulated.
128 devices in a mesh: row: 4 (over x), col: 32 (over z, y, core).
Axes of the slice: x: 4, y: 4, z: 4, core: 2. Of those that a mesh axis runs over, the one named last changes fastest.
Arguments:
- child_factors: bfloat16 [2, 2048, 8192], P(None, 'col', 'row'), may hold values from -0.0625 to 0.0625
- child_tiles: int32 [2, 16], replicated, may hold values from 0 to 63, as said below
- root_diag: float32 [8192], P('col'), may hold values from 0.5 to 4
Outputs:
- front_out: float32 [8192, 8192], P('row', 'col')
Inputs may be any that keep to these rules, and one draw needn't show every extreme that they name: `child_tiles`: each row lists 2048 / 128 distinct root tiles in increasing order; the first child's list holds tile 0 and the second child's holds the last tile. For every r below 4, exactly 2048 / (128 * 4) tiles t of each row have ((t * 128) // 256) % 4 == r.
All inputs are finite; a program needn't handle non-finite values.
Results may differ from a plain program's by a relative error of at most 0.0003.
Values may be sent and summed in bfloat16 or wider, within the bound.
No kernel may reach another device: no remote copies, remote signals or barrier semaphores. Data moves between devices by JAX's collectives and lax.ppermute only.
A program may use at most 128 MiB of HBM per device.

v0:
```python
import jax
import jax.numpy as jnp
from jax import lax
from jax.sharding import PartitionSpec as P

TILE = 128
NPAN = 1


def broadcast(block, axis, source):
    block = jnp.where(lax.axis_index(axis) == source, block, jnp.zeros_like(block))
    return lax.psum(block, axis)


def pivot_factor(source, local_block, owner_row, block_size, identity, usable):
    diag_rows = source[local_block * block_size : (local_block + 1) * block_size]
    pivots = broadcast(diag_rows, "row", owner_row)
    return jnp.linalg.cholesky(jnp.where(usable, pivots, identity))


def solve_panel(source, factor, row_block, panel_step, blocks_here):
    solved = lax.linalg.triangular_solve(
        factor, source, left_side=False, lower=True, transpose_a=True
    )
    repeated = jnp.tile(jnp.tril(factor), (blocks_here, 1))
    later = (row_block > panel_step)[:, None]
    current = (row_block == panel_step)[:, None]
    return jnp.where(later, solved, jnp.where(current, repeated, 0.0))


def shards(child_factors, child_tiles, root_diag):
    highest = lax.Precision.HIGHEST
    row_count = lax.axis_size("row")
    col_count = lax.axis_size("col")
    block_size = root_diag.shape[0]
    order_total = block_size * col_count
    loc_rows = order_total // row_count
    blocks_here = loc_rows // block_size
    row_index = lax.axis_index("row")
    col_index = lax.axis_index("col")
    gathered = lax.all_gather(child_factors, "col", axis=1, tiled=True)
    tile_total = gathered.shape[1] // TILE
    tiles_per_col = block_size // TILE
    wanted = col_index * tiles_per_col + jnp.arange(tiles_per_col, dtype=jnp.int32)
    selector = (child_tiles[:, :, None] == wanted[None, None, :]).astype(jnp.bfloat16)
    tiled_rows = gathered.reshape(2, tile_total, TILE, gathered.shape[2])
    own_cols = jnp.einsum(
        "cui,cutk->citk", selector, tiled_rows, preferred_element_type=jnp.float32
    )
    own_cols = own_cols.astype(jnp.bfloat16).reshape(2, block_size, gathered.shape[2])
    partial_gram = jnp.einsum(
        "cnk,cmk->cnm", gathered, own_cols, preferred_element_type=jnp.float32
    )
    gram_tiles = partial_gram.reshape(2, tile_total, TILE, block_size)
    stored_tile = jnp.arange(lax.axis_size("row") * loc_rows // TILE, dtype=jnp.int32)
    stored_row = stored_tile * TILE
    owning = stored_row // loc_rows
    within = stored_row % loc_rows
    global_row = (owning + within // block_size * row_count) * block_size + within % block_size
    global_tile = global_row // TILE
    matches = (child_tiles[:, :, None] == global_tile[None, None, :]).astype(jnp.float32)
    placed = jnp.einsum("cus,cutm->stm", matches, gram_tiles, precision=highest)
    assembled = lax.psum_scatter(
        placed.reshape(lax.axis_size("row") * loc_rows, block_size),
        "row",
        scatter_dimension=0,
        tiled=True,
    )
    local_rows = jnp.arange(loc_rows, dtype=jnp.int32)
    row_block = row_index + local_rows // block_size * row_count
    glob_rows = row_block * block_size + local_rows % block_size
    glob_cols = col_index * block_size + jnp.arange(block_size, dtype=jnp.int32)
    front_now = assembled + jnp.where(
        glob_rows[:, None] == glob_cols[None, :], root_diag[None, :], 0.0
    )
    identity = jnp.eye(block_size, dtype=jnp.float32)
    owner_row = 0 % row_count
    local_block = 0 // row_count
    factor = pivot_factor(front_now, local_block, owner_row, block_size, identity, col_index == 0)
    own_panel = solve_panel(front_now, factor, row_block, 0, blocks_here)
    panel_block = broadcast(own_panel, "col", 0)
    own_block = lax.dynamic_slice_in_dim(
        panel_block, col_index // row_count * block_size, block_size, 0
    )
    across = broadcast(own_block.astype(jnp.bfloat16), "row", col_index % row_count).astype(
        own_block.dtype
    )
    update = jnp.dot(panel_block, across.T, precision=highest)
    front_now = jnp.where(col_index == 0, panel_block, front_now - update)
    upper_part = (row_block[:, None] < NPAN) & (col_index >= NPAN)
    return jnp.where(upper_part, 0.0, front_now)


def solution(mesh):
    placed = (P(None, "col", "row"), P(), P("col"))
    return jax.shard_map(
        shards, mesh=mesh, in_specs=placed, out_specs=P("row", "col"), check_vma=False
    )
```

profile of v0, /device:TPU:0, one launch (start us, length us, event | category | flops | bytes accessed | tf_op | source)
XLA Modules:
  0.0 501.5 jit_solution(1409809897628505502)
XLA Ops:
  7.4 77.5 %all-gather.2.cloned.1.call-done = bf16[2,2048,2048]{2,1,0:T(8,128)(2,1)} async-done(((bf16[2,64,2048]{2,1,0:T(8,128)(2,1)}), bf16[2,2048,2048]{2,1,0:T(8,128)(2,1)}) %all-gather.2.cloned.1.call-update) | async-done | bytes 16777232 | tf_op jit(solution)/shard_map/all_gather | solution.py:41
  84.8 24.6 %fusion.2 = bf16[2,2,128,2048]{3,1,2,0:T(2,128)(2,1)S(1)} fusion(bf16[2,16,128,2048]{3,2,1,0:T(8,128)(2,1)} %bitcast.68, s32[2,16]{1,0:T(2,128)} %param.4, s32[2]{0:T(128)S(1)} %iota_add_fusion.1), kind=kOutput, calls=%fused_computation.5 | convolution fusion | flops 34603072 | bytes 18874504 | tf_op jit(solution)/shard_map/cui,cutk->citk/dot_general | solution.py:47
  109.5 2.2 copy.14
  111.7 13.0 %fusion.43 = f32[2,256,2048]{2,1,0:T(8,128)} fusion(bf16[2,256,2048]{2,1,0:T(8,128)(2,1)} %bitcast.73, bf16[2,2048,2048]{2,1,0:T(8,128)(2,1)} %all-gather.2.cloned.1.call-done), kind=kOutput, calls=%fused_computation.88 | convolution fusion | flops 4294967296 | bytes 23068672 | tf_op jit(solution)/shard_map/cnk,cmk->cnm/dot_general | solution.py:51
  124.7 3.1 copy.31
  127.9 3.6 fusion.21
  131.5 11.1 %copy.39 = f32[32,8,64,128]{3,1,2,0:T(8,128)} copy(f32[32,8,64,128]{3,2,1,0:T(8,128)S(1)} %bitcast.67) | data formatting | bytes 16777216
  142.7 80.0 %reduce-scatter.2.cloned.1.call-done = f32[2048,256]{0,1:T(8,128)} async-done(((f32[8192,256]{0,1:T(8,128)}), f32[2048,256]{0,1:T(8,128)}) %reduce-scatter.2.cloned.1.call-update) | async-done | bytes 2097168 | tf_op jit(solution)/shard_map/reduce_scatter | solution.py:63
  222.7 1.9 select_add_fusion
  225.4 41.6 %all-reduce.5.cloned.1.call-done = f32[256,256]{0,1:T(8,128)} async-done(((f32[256,256]{0,1:T(8,128)}), f32[256,256]{0,1:T(8,128)}) %all-reduce.5.cloned.1.call-update) | async-done | bytes 262160 | tf_op jit(solution)/shard_map/psum | solution.py:12
  269.1 11.7 %cholesky.49 = f32[128,128]{1,0:T(8,128)S(1)} custom-call(f32[128,128]{1,0:T(8,128)S(1)} %cholesky.115), custom_call_target="Cholesky" | custom-call | tf_op jit(solution)/shard_map/jit(cholesky)/cholesky | solution.py:18
  280.8 9.8 %custom-call.14 = f32[1,128,128]{1,2,0:T(8,128)S(1)} custom-call(f32[1,128,128]{2,1,0:T(8,128)S(1)} %get-tuple-element.32), custom_call_target="InvertDiagBlocksLowerTriangular" | custom-call | tf_op jit(solution)/shard_map/jit(cholesky)/cholesky | solution.py:18
  291.1 11.7 %cholesky.103 = f32[128,128]{1,0:T(8,128)S(1)} custom-call(f32[128,128]{1,0:T(8,128)S(1)} %convolution_subtract_fusion.2), custom_call_target="Cholesky" | custom-call | tf_op jit(solution)/shard_map/jit(cholesky)/cholesky | solution.py:18
  305.5 2.2 copy.33
  307.8 4.5 while.1
  308.7 1.3 dynamic-slice.7
  310.8 1.3 dynamic-slice.7
  312.3 19.7 %custom-call.15 = f32[2,128,128]{1,2,0:T(8,128)S(1)} custom-call(f32[2,128,128]{2,1,0:T(8,128)S(1)} %get-tuple-element.12), custom_call_target="InvertDiagBlocksLowerTriangular" | custom-call | tf_op jit(solution)/shard_map/triangular_solve | solution.py:22
  335.3 1.7 fusion.7
  337.1 106.4 %all-reduce.7.cloned.1.call-done = f32[2048,256]{0,1:T(8,128)} async-done(((f32[2048,256]{0,1:T(8,128)}), f32[2048,256]{0,1:T(8,128)}) %all-reduce.7.cloned.1.call-update) | async-done | bytes 2097168 | tf_op jit(solution)/shard_map/psum | solution.py:12
  443.5 1.6 fusion.11
  445.1 41.5 %all-reduce.9.cloned.1.call-done = bf16[256,256]{0,1:T(8,128)(2,1)} async-done(((bf16[256,256]{0,1:T(8,128)(2,1)}), bf16[256,256]{0,1:T(8,128)(2,1)}) %all-reduce.9.cloned.1.call-update) | async-done | bytes 131088 | tf_op jit(solution)/shard_map/psum | solution.py:12
  486.7 5.0 fusion.6
  491.6 2.9 copy.23
  (54 shorter events, 10.5 us)
Async XLA Ops:
  6.5 78.3 %all-gather.2.cloned.1.call-start = ((), (), s32[]{:S(2)}) async-start(), calls=%async_computation.1 | async-start | bytes 17301504 | tf_op jit(solution)/shard_map/all_gather | solution.py:41
  7.3 215.4 %reduce-scatter.2.cloned.1.call-start = ((), (), s32[]{:S(2)}) async-start(), calls=%async_computation.2 | async-start | bytes 10485760 | tf_op jit(solution)/shard_map/reduce_scatter | solution.py:63
  124.7 3.1 copy-start.1
  142.6 80.1 %copy-start.2 = (f32[256]{0:T(256)S(1)}, f32[256]{0:T(256)}, u32[]{:S(2)}) copy-start(f32[256]{0:T(256)} %param.5) | copy-start | bytes 3076
  142.6 124.4 %all-reduce.5.cloned.1.call-start = ((), (), s32[]{:S(2)}) async-start(), calls=%async_computation.3 | async-start | bytes 524288 | tf_op jit(solution)/shard_map/psum | solution.py:12
  225.3 218.2 %all-reduce.7.cloned.1.call-start = ((), (), s32[]{:S(2)}) async-start(), calls=%async_computation.4 | async-start | bytes 4194304 | tf_op jit(solution)/shard_map/psum | solution.py:12
  333.1 2.2 copy-start
  337.0 149.7 %all-reduce.9.cloned.1.call-start = ((), (), s32[]{:S(2)}) async-start(), calls=%async_computation.5 | async-start | bytes 262144 | tf_op jit(solution)/shard_map/psum | solution.py:12
Sparse Core Ops, SparseCore 0:
  9.6 75.1 all-gather.1
  142.7 79.8 reduce-scatter.1
  225.4 41.5 all-reduce.4
  337.1 106.3 all-reduce.6
  445.6 40.9 all-reduce.8
where the time goes:
time: 510 us; the launch traced here: 501 us
  waiting for transfers between devices  348 us (68%)
  other arithmetic  61.7 us (12%)
  matrix products  50 us (10%)
  local copies, waits for them, and re-layouts  26.4 us (5%)
  between operations  15.2 us (3%)
    psum x3, waiting for transfers between devices, broadcast(): return lax.psum(block, axis)  190 us
    reduce_scatter x1, waiting for transfers between devices, shards(): lax.psum_scatter(placed.reshape(lax.axis_size('row') * loc_rows, block_si...  80 us
    all_gather x1, waiting for transfers between devices, shards(): gathered = lax.all_gather(child_factors, 'col', axis=1, tiled=True)  77.5 us
    another operation x6, other arithmetic, pivot_factor(): return jnp.linalg.cholesky(jnp.where(usable, pivots, identity))  34 us
    dot_general x1, matrix products, shards(): jnp.einsum('cui,cutk->citk', selector, tiled_rows, preferred_element_type...  24.6 us
    another operation x3, other arithmetic, solve_panel(): lax.linalg.triangular_solve(factor, source, left_side=False, lower=True,...  19.7 us
    unnamed x9, local copies, waits for them, and re-layouts  16.4 us
    dot_general x1, matrix products, shards(): jnp.einsum('cnk,cmk->cnm', gathered, own_cols, preferred_element_type=jnp...  13 us
  transfers between devices with their start and end apart: 5, of which 5 were waited for; matrix products, arithmetic and copies ran while one was open for 0% of the time, Pallas kernels for 0%

commit v1 on v0

--- a/solution.py
+++ b/solution.py
@@ -38,7 +38,9 @@
     blocks_here = loc_rows // block_size
     row_index = lax.axis_index("row")
     col_index = lax.axis_index("col")
-    gathered = lax.all_gather(child_factors, "col", axis=1, tiled=True)
+    gathered = jnp.concatenate(
+        lax.all_to_all(jnp.stack([child_factors] * lax.axis_size("col")), "col", 0, 0), axis=1
+    )
     tile_total = gathered.shape[1] // TILE
     tiles_per_col = block_size // TILE
     wanted = col_index * tiles_per_col + jnp.arange(tiles_per_col, dtype=jnp.int32)

time: 510 us -> 672 us (1.32)
  waiting for transfers between devices: 348 us -> 480 us
  local copies, waits for them, and re-layouts: 26.4 us -> 46 us
  starting transfers between devices: 0.17 us -> 8.74 us
    all_to_all x0 -> x1, waiting for transfers between devices: none -> 213 us  [shards(): lax.all_to_all(jnp.stack([child_factors] * lax.axis_size('col')), 'col',...]
    all_gather x1 -> x0, waiting for transfers between devices: 77.5 us -> none  [shards(): gathered = lax.all_gather(child_factors, 'col', axis=1, tiled=True)]
    all_to_all x0 -> x1, local copies, waits for them, and re-layouts: none -> 14.1 us  [shards(): lax.all_to_all(jnp.stack([child_factors] * lax.axis_size('col')), 'col',...]
    all_to_all x0 -> x1, starting transfers between devices: none -> 8.57 us  [shards(): lax.all_to_all(jnp.stack([child_factors] * lax.axis_size('col')), 'col',...]
    another operation x10 -> x11, local copies, waits for them, and re-layouts: 4.22 us -> 11 us  [the longest x1 6.78 us: shards(): jnp.stack([child_factors] * lax.axis_size('col'))]
    unnamed x9 -> x7, local copies, waits for them, and re-layouts: 16.4 us -> 15.1 us
where the time goes in v1:
time: 672 us; the launch traced here: 662 us
  waiting for transfers between devices  480 us (71%)
  other arithmetic  61.7 us (9%)
  matrix products  50 us (7%)
  local copies, waits for them, and re-layouts  46 us (7%)
  between operations  15.2 us (2%)
  starting transfers between devices  8.74 us (1%)
    all_to_all x1, waiting for transfers between devices, shards(): lax.all_to_all(jnp.stack([child_factors] * lax.axis_size('col')), 'col',...  213 us
    psum x3, waiting for transfers between devices, broadcast(): return lax.psum(block, axis)  189 us
    reduce_scatter x1, waiting for transfers between devices, shards(): lax.psum_scatter(placed.reshape(lax.axis_size('row') * loc_rows, block_si...  77.3 us
    another operation x6, other arithmetic, pivot_factor(): return jnp.linalg.cholesky(jnp.where(usable, pivots, identity))  34 us
    dot_general x1, matrix products, shards(): jnp.einsum('cui,cutk->citk', selector, tiled_rows, preferred_element_type...  24.6 us
    another operation x3, other arithmetic, solve_panel(): lax.linalg.triangular_solve(factor, source, left_side=False, lower=True,...  19.7 us
    unnamed x7, local copies, waits for them, and re-layouts  15.1 us
    all_to_all x1, local copies, waits for them, and re-layouts, shards(): lax.all_to_all(jnp.stack([child_factors] * lax.axis_size('col')), 'col',...  14.1 us
  transfers between devices with their start and end apart: 5, of which 5 were waited for; matrix products, arithmetic and copies ran while one was open for 0% of the time, Pallas kernels for 0%

profile of v1, /device:TPU:0, one launch (start us, length us, event | category | flops | bytes accessed | tf_op | source)
XLA Modules:
  0.0 661.9 jit_solution(3184293651896352353)
XLA Ops:
  6.5 6.8 %stack.2 = bf16[32,2,64,2048]{3,2,1,0:T(8,128)(2,1)} broadcast(bf16[2,64,2048]{2,1,0:T(8,128)(2,1)} %param.3), dimensions={1,2,3} | broadcast | bytes 17301504 | tf_op jit(solution)/shard_map/stack | solution.py:42
  13.3 8.6 %all-to-all-start = ((bf16[32,2,64,2048]{3,2,1,0:T(8,128)(2,1)}), bf16[32,2,64,2048]{3,2,1,0:T(8,128)(2,1)}, u32[]{:S(2)}, u32[]{:S(2)}) async-start(bf16[32,2,64,2048]{3,2,1,0:T(8,128)(2,1)} %stack.2), calls=%async_computation | async-start | bytes 33554432 | tf_op jit(solution)/shard_map/all_to_all | solution.py:42
  22.0 213.1 %all-to-all-done = bf16[32,2,64,2048]{3,2,1,0:T(8,128)(2,1)} async-done(((bf16[32,2,64,2048]{3,2,1,0:T(8,128)(2,1)}), bf16[32,2,64,2048]{3,2,1,0:T(8,128)(2,1)}, u32[]{:S(2)}, u32[]{:S(2)}) %all-to-all-start) | async-done | bytes 16777248 | tf_op jit(solution)/shard_map/all_to_all | solution.py:42
  235.2 14.1 %copy.24 = bf16[32,2,64,2048]{3,2,0,1:T(8,128)(2,1)} copy(bf16[32,2,64,2048]{3,2,1,0:T(8,128)(2,1)} %all-to-all-done) | data formatting | bytes 33554432 | tf_op jit(solution)/shard_map/all_to_all | solution.py:42
  249.3 24.6 %fusion.2 = bf16[2,2,128,2048]{3,1,2,0:T(2,128)(2,1)S(1)} fusion(bf16[2,16,128,2048]{3,2,1,0:T(8,128)(2,1)} %bitcast.70, s32[2,16]{1,0:T(2,128)S(1)} %copy-done, s32[2]{0:T(128)S(1)} %iota_add_fusion.1), kind=kOutput, calls=%fused_computation.5 | convolution fusion | flops 34603072 | bytes 18874504 | tf_op jit(solution)/shard_map/cui,cutk->citk/dot_general | solution.py:49
  273.9 2.2 copy.26
  276.1 13.0 %fusion.43 = f32[2,256,2048]{2,1,0:T(8,128)} fusion(bf16[2,256,2048]{2,1,0:T(8,128)(2,1)} %bitcast.78, bf16[2,2048,2048]{2,1,0:T(8,128)(2,1)} %bitcast.71), kind=kOutput, calls=%fused_computation.88 | convolution fusion | flops 4294967296 | bytes 23068672 | tf_op jit(solution)/shard_map/cnk,cmk->cnm/dot_general | solution.py:53
  289.1 3.1 copy.45
  292.3 3.6 fusion.21
  295.9 11.1 %copy.53 = f32[32,8,64,128]{3,1,2,0:T(8,128)} copy(f32[32,8,64,128]{3,2,1,0:T(8,128)S(1)} %bitcast.73) | data formatting | bytes 16777216
  307.1 77.3 %reduce-scatter.2.cloned.1.call-done = f32[2048,256]{0,1:T(8,128)} async-done(((f32[8192,256]{0,1:T(8,128)}), f32[2048,256]{0,1:T(8,128)}) %reduce-scatter.2.cloned.1.call-update) | async-done | bytes 2097168 | tf_op jit(solution)/shard_map/reduce_scatter | solution.py:65
  384.4 1.9 select_add_fusion
  387.2 41.6 %all-reduce.5.cloned.1.call-done = f32[256,256]{0,1:T(8,128)} async-done(((f32[256,256]{0,1:T(8,128)}), f32[256,256]{0,1:T(8,128)}) %all-reduce.5.cloned.1.call-update) | async-done | bytes 262160 | tf_op jit(solution)/shard_map/psum | solution.py:12
  430.9 11.7 %cholesky.49 = f32[128,128]{1,0:T(8,128)S(1)} custom-call(f32[128,128]{1,0:T(8,128)S(1)} %cholesky.115), custom_call_target="Cholesky" | custom-call | tf_op jit(solution)/shard_map/jit(cholesky)/cholesky | solution.py:18
  442.7 9.8 %custom-call.14 = f32[1,128,128]{1,2,0:T(8,128)S(1)} custom-call(f32[1,128,128]{2,1,0:T(8,128)S(1)} %get-tuple-element.36), custom_call_target="InvertDiagBlocksLowerTriangular" | custom-call | tf_op jit(solution)/shard_map/jit(cholesky)/cholesky | solution.py:18
  453.1 11.7 %cholesky.103 = f32[128,128]{1,0:T(8,128)S(1)} custom-call(f32[128,128]{1,0:T(8,128)S(1)} %convolution_subtract_fusion.2), custom_call_target="Cholesky" | custom-call | tf_op jit(solution)/shard_map/jit(cholesky)/cholesky | solution.py:18
  467.2 4.6 while.1
  471.8 19.7 %custom-call.15 = f32[2,128,128]{1,2,0:T(8,128)S(1)} custom-call(f32[2,128,128]{2,1,0:T(8,128)S(1)} %get-tuple-element.12), custom_call_target="InvertDiagBlocksLowerTriangular" | custom-call | tf_op jit(solution)/shard_map/triangular_solve | solution.py:22
  495.7 1.7 fusion.7
  497.5 106.3 %all-reduce.7.cloned.1.call-done = f32[2048,256]{0,1:T(8,128)} async-done(((f32[2048,256]{0,1:T(8,128)}), f32[2048,256]{0,1:T(8,128)}) %all-reduce.7.cloned.1.call-update) | async-done | bytes 2097168 | tf_op jit(solution)/shard_map/psum | solution.py:12
  603.9 1.6 fusion.11
  605.5 41.5 %all-reduce.9.cloned.1.call-done = bf16[256,256]{0,1:T(8,128)(2,1)} async-done(((bf16[256,256]{0,1:T(8,128)(2,1)}), bf16[256,256]{0,1:T(8,128)(2,1)}) %all-reduce.9.cloned.1.call-update) | async-done | bytes 131088 | tf_op jit(solution)/shard_map/psum | solution.py:12
  647.1 5.0 fusion.6
  652.0 2.9 copy.36
  (53 shorter events, 13.3 us)
Async XLA Ops:
  13.3 221.8 %all-to-all-start = ((bf16[32,2,64,2048]{3,2,1,0:T(8,128)(2,1)}), bf16[32,2,64,2048]{3,2,1,0:T(8,128)(2,1)}, u32[]{:S(2)}, u32[]{:S(2)}) async-start(bf16[32,2,64,2048]{3,2,1,0:T(8,128)(2,1)} %stack.2), calls=%async_computation | async-start | bytes 33554432 | tf_op jit(solution)/shard_map/all_to_all | solution.py:42
  21.9 362.5 %reduce-scatter.2.cloned.1.call-start = ((), (), s32[]{:S(2)}) async-start(), calls=%async_computation.2 | async-start | bytes 10485760 | tf_op jit(solution)/shard_map/reduce_scatter | solution.py:65
  22.0 227.3 %copy-start = (s32[2,16]{1,0:T(2,128)S(1)}, s32[2,16]{1,0:T(2,128)}, u32[]{:S(2)}) copy-start(s32[2,16]{1,0:T(2,128)} %param.4) | copy-start | bytes 388
  307.0 77.5 %copy-start.1 = (f32[256]{0:T(256)S(1)}, f32[256]{0:T(256)}, u32[]{:S(2)}) copy-start(f32[256]{0:T(256)} %param.5) | copy-start | bytes 3076
  307.0 121.7 %all-reduce.5.cloned.1.call-start = ((), (), s32[]{:S(2)}) async-start(), calls=%async_computation.3 | async-start | bytes 524288 | tf_op jit(solution)/shard_map/psum | solution.py:12
  387.1 216.8 %all-reduce.7.cloned.1.call-start = ((), (), s32[]{:S(2)}) async-start(), calls=%async_computation.4 | async-start | bytes 4194304 | tf_op jit(solution)/shard_map/psum | solution.py:12
  497.4 149.6 %all-reduce.9.cloned.1.call-start = ((), (), s32[]{:S(2)}) async-start(), calls=%async_computation.5 | async-start | bytes 262144 | tf_op jit(solution)/shard_map/psum | solution.py:12
Sparse Core Ops, SparseCore 0:
  307.1 77.2 reduce-scatter.1
  387.2 41.4 all-reduce.4
  497.6 106.2 all-reduce.6
  606.0 40.9 all-reduce.8
